TPU v7x, 512 devices: a whole 4x4x16 slice. The times are simulated.
512 devices in a mesh: ctx: 16 (over z), ep: 32 (over y, x, core).
Axes of the slice: x: 4, y: 4, z: 16, core: 2. Of those that a mesh axis runs over, the one named last changes fastest.
Arguments:
- query_act: bfloat16 [2048, 8192], P('ctx', 'ep'), may hold values from -6 to 6
- key_act: bfloat16 [2048, 8192], P('ctx', 'ep'), may hold values from -6 to 6
- value_act: bfloat16 [2048, 8192], P('ctx', 'ep'), may hold values from -6 to 6
- state_init: float32 [64, 128, 128], P('ep'), may hold values from -128 to 128
- head_gain: float32 [8192], P('ep'), may hold values from 0.25 to 1.75
- out_weight: bfloat16 [8192, 3072], P('ctx', 'ep'), may hold values from -0.0625 to 0.0625
- stream_in: bfloat16 [2048, 3072], P('ctx', 'ep'), may hold values from -150 to 150
- model_gain: float32 [3072], replicated, may hold values from 0.25 to 1.75
- expert_ids: int32 [2048, 2], P('ctx'), may hold values from 0 to 15, as said below
- expert_slots: int32 [2048, 2], P('ctx'), may hold values from 0 to 19, as said below
- route_gates: float32 [2048, 2], P('ctx'), may hold values from 0.2 to 1
- gate_weight: bfloat16 [32, 3072, 3072], P('ep', 'ctx'), may hold values from -0.109375 to 0.109375
- up_weight: bfloat16 [32, 3072, 3072], P('ep', 'ctx'), may hold values from -0.109375 to 0.109375
- down_weight: bfloat16 [32, 3072, 3072], P('ep', 'ctx'), may hold values from -0.078125 to 0.078125
- out_grad: bfloat16 [2048, 3072], P('ctx', 'ep'), may hold values from -6 to 6
Outputs:
- layer_out: bfloat16 [2048, 3072], P('ctx', 'ep')
- grad_query: bfloat16 [2048, 8192], P('ctx', 'ep')
- grad_key: bfloat16 [2048, 8192], P('ctx', 'ep')
- grad_value: bfloat16 [2048, 8192], P('ctx', 'ep')
- grad_state: float32 [64, 128, 128], P('ep')
- grad_stream: bfloat16 [2048, 3072], P('ctx', 'ep')
Inputs may be any that keep to these rules, and one draw needn't show every extreme that they name: `expert_ids`: within each block of 128 tokens a token's two experts differ; the tokens naming expert e hold the slots 0 to n - 1 of e once each, n being their number; no expert is named by more than 20 tokens of a block, and in every block some expert by exactly 20. `expert_slots`: see expert_ids.
All inputs are finite; a program needn't handle non-finite values.
Results may differ from a plain program's by a relative error of at most 0.02.
Values may be sent and summed in bfloat16 or wider, within the bound.
No kernel may reach another device: no remote copies, remote signals or barrier semaphores. Data moves between devices by JAX's collectives and lax.ppermute only.
A program may use at most 64 MiB of HBM per device.

v0:
```python
import jax
import jax.numpy as jnp
from jax import lax
from jax.sharding import PartitionSpec as P


def carried_in(value, axis, join, neutral, backward):
    count = lax.axis_size(axis)
    place = lax.axis_index(axis)
    ahead = count - 1 - place if backward else place
    gathered = lax.all_gather(value.astype(jnp.bfloat16), axis)
    state = jnp.zeros_like(value) + jnp.asarray(neutral, value.dtype)

    def one(turn, state):
        source = count - 1 - turn if backward else turn
        return join(state, lax.dynamic_index_in_dim(gathered, source, 0, False).astype(value.dtype))

    return lax.fori_loop(0, ahead, one, state)


def head_normalize(attended, gain):
    factor = lax.rsqrt(jnp.mean(attended * attended, -1, keepdims=True) + 1e-06)
    return attended * factor * gain


def add_states(earlier, later_one):
    return earlier + later_one


def contract_last(left, right):
    return lax.dot_general(
        left, right, (((1,), (1,)), ((), ())), preferred_element_type=jnp.float32
    )


def local(
    query_act,
    key_act,
    value_act,
    state_init,
    head_gain,
    out_weight,
    stream_in,
    model_gain,
    expert_ids,
    expert_slots,
    route_gates,
    gate_weight,
    up_weight,
    down_weight,
    out_grad,
):
    f32 = jnp.float32
    high = lax.Precision.HIGHEST
    ep_count = lax.axis_size("ep")
    expert_count = ep_count // 2
    my_ep = lax.axis_index("ep")
    tokens_here = query_act.shape[0]
    head_count = state_init.shape[0]
    head_size = state_init.shape[1]
    model_width = model_gain.shape[0]
    columns = stream_in.shape[1]
    capacity = 5 * tokens_here // (2 * expert_count)
    query3 = query_act.reshape(tokens_here, head_count, head_size)
    key3 = key_act.reshape(tokens_here, head_count, head_size)
    value3 = value_act.reshape(tokens_here, head_count, head_size)
    kv_own = jnp.einsum("thd,the->hde", key3, value3, preferred_element_type=f32)
    zero_state = jnp.zeros_like(kv_own)
    before = carried_in(kv_own, "ctx", add_states, zero_state, False)
    prefix = state_init + before
    causal = jnp.arange(tokens_here)[:, None] >= jnp.arange(tokens_here)[None, :]
    scores = jnp.einsum("thd,shd->hts", query3, key3, preferred_element_type=f32)
    scores_bf = jnp.where(causal[None], scores, 0.0).astype(jnp.bfloat16)
    inside = jnp.einsum("hts,she->the", scores_bf, value3, preferred_element_type=f32)
    from_state = jnp.einsum("thd,hde->the", query3.astype(f32), prefix, precision=high)
    attended = from_state + inside
    gain_heads = head_gain.reshape(head_count, head_size)
    normed_heads = (
        head_normalize(attended, gain_heads)
        .astype(jnp.bfloat16)
        .reshape(tokens_here, head_count * head_size)
    )
    w_cols = lax.all_gather(out_weight, "ctx", axis=0, tiled=True)
    attn_proj = jnp.dot(
        lax.all_gather(normed_heads, "ep", axis=1, tiled=True), w_cols, preferred_element_type=f32
    )
    stream = (stream_in.astype(f32) + attn_proj).astype(jnp.bfloat16)
    stream_f = stream.astype(f32)
    gain_cols = lax.dynamic_slice_in_dim(model_gain, my_ep * columns, columns, 0)
    dest_expert = jnp.arange(ep_count) % expert_count
    slot_iota = jnp.arange(capacity)
    hits = (expert_ids[:, :, None, None] == dest_expert[None, None, :, None]) & (
        expert_slots[:, :, None, None] == slot_iota[None, None, None, :]
    )
    hits_f = hits.astype(f32)
    dest_picks = jnp.sum(hits_f, 1).reshape(tokens_here, ep_count * capacity)
    dest_weights = jnp.sum(hits_f * route_gates[:, :, None, None], 1).reshape(
        tokens_here, ep_count * capacity
    )
    whole_rows = lax.all_gather(stream, "ep", axis=1, tiled=True).astype(f32)
    row_scale = lax.rsqrt(jnp.mean(whole_rows * whole_rows, -1, keepdims=True) + 1e-05)
    model_in = (whole_rows * row_scale * model_gain).astype(jnp.bfloat16)
    own_select = lax.dynamic_slice_in_dim(dest_picks, my_ep * capacity, capacity, 1).T.astype(
        jnp.bfloat16
    )
    expert_in = jnp.dot(own_select, model_in, preferred_element_type=f32).astype(jnp.bfloat16)
    w_gate = gate_weight[0]
    w_up = up_weight[0]
    w_down = down_weight[0]
    hidden_block = w_gate.shape[0]
    portion = lax.all_gather(expert_in, "ctx", axis=0, tiled=True)
    projected = jnp.concatenate([contract_last(portion, w_gate), contract_last(portion, w_up)], 1)
    pre_gate = projected[:, :hidden_block]
    pre_up = projected[:, hidden_block:]
    gate_sig = jax.nn.sigmoid(pre_gate)
    activated = (pre_gate * gate_sig * pre_up).astype(jnp.bfloat16)
    half_out = lax.psum_scatter(
        jnp.dot(activated, w_down, preferred_element_type=f32).astype(jnp.bfloat16),
        "ctx",
        scatter_dimension=0,
        tiled=True,
    )
    returned = lax.all_to_all(half_out, "ep", split_axis=1, concat_axis=0, tiled=True)
    expert_mix = jnp.dot(dest_weights, returned.astype(f32), precision=high)
    layer_out = (stream_f + expert_mix).astype(jnp.bfloat16)
    grad_out = out_grad.astype(f32)
    grad_send = jnp.dot(dest_weights.T, grad_out, precision=high).astype(jnp.bfloat16)
    grad_in = lax.all_to_all(grad_send, "ep", split_axis=0, concat_axis=1, tiled=True)
    grad_act = contract_last(lax.all_gather(grad_in, "ctx", axis=0, tiled=True), w_down)
    grad_gate_pre = (grad_act * pre_up * gate_sig * (1.0 + pre_gate * (1.0 - gate_sig))).astype(
        jnp.bfloat16
    )
    grad_up_pre = (grad_act * pre_gate * gate_sig).astype(jnp.bfloat16)
    grad_half = lax.psum_scatter(
        (
            jnp.dot(grad_gate_pre, w_gate, preferred_element_type=f32)
            + jnp.dot(grad_up_pre, w_up, preferred_element_type=f32)
        ).astype(jnp.bfloat16),
        "ctx",
        scatter_dimension=0,
        tiled=True,
    )
    grad_back = lax.all_to_all(grad_half, "ep", split_axis=1, concat_axis=0, tiled=True)
    grad_model_in = jnp.dot(dest_picks, grad_back.astype(f32), precision=high)
    scaled_grad = grad_model_in * gain_cols
    inner_sum = lax.psum(jnp.sum(stream_f * scaled_grad, -1), "ep")
    grad_stream = (
        grad_out
        + row_scale * scaled_grad
        - stream_f * row_scale**3 * inner_sum[:, None] / model_width
    ).astype(jnp.bfloat16)
    w_rows = lax.all_to_all(w_cols, "ep", split_axis=0, concat_axis=1, tiled=True)
    grad_heads = contract_last(lax.all_gather(grad_stream, "ep", axis=1, tiled=True), w_rows)
    head_pull = jax.vjp(lambda value: head_normalize(value, gain_heads), attended)[1]
    grad_attended = head_pull(grad_heads.reshape(tokens_here, head_count, head_size))[0].astype(
        jnp.bfloat16
    )
    state_part = jnp.einsum("thd,the->hde", query3, grad_attended, preferred_element_type=f32)
    later_sum = carried_in(state_part, "ctx", add_states, zero_state, True)
    state_total = lax.psum(state_part.astype(jnp.bfloat16), "ctx").astype(jnp.float32)
    grad_scores = jnp.einsum("the,she->hts", grad_attended, value3, preferred_element_type=f32)
    grad_masked = jnp.where(causal[None], grad_scores, 0.0).astype(jnp.bfloat16)
    grad_att_f = grad_attended.astype(f32)
    grad_query = jnp.einsum("the,hde->thd", grad_att_f, prefix, precision=high) + jnp.einsum(
        "hts,shd->thd", grad_masked, key3, preferred_element_type=f32
    )
    grad_key = jnp.einsum(
        "the,hde->thd", value3.astype(f32), later_sum, precision=high
    ) + jnp.einsum("hts,thd->shd", grad_masked, query3, preferred_element_type=f32)
    grad_value = jnp.einsum(
        "thd,hde->the", key3.astype(f32), later_sum, precision=high
    ) + jnp.einsum("hts,the->she", scores_bf, grad_attended, preferred_element_type=f32)
    flat_shape = (tokens_here, head_count * head_size)
    return (
        layer_out,
        grad_query.astype(jnp.bfloat16).reshape(flat_shape),
        grad_key.astype(jnp.bfloat16).reshape(flat_shape),
        grad_value.astype(jnp.bfloat16).reshape(flat_shape),
        state_total,
        grad_stream,
    )


def solution(mesh):
    return jax.shard_map(
        local,
        mesh=mesh,
        in_specs=(
            P("ctx", "ep"),
            P("ctx", "ep"),
            P("ctx", "ep"),
            P("ep", None, None),
            P("ep"),
            P("ctx", "ep"),
            P("ctx", "ep"),
            P(),
            P("ctx", None),
            P("ctx", None),
            P("ctx", None),
            P("ep", "ctx", None),
            P("ep", "ctx", None),
            P("ep", "ctx", None),
            P("ctx", "ep"),
        ),
        out_specs=(
            P("ctx", "ep"),
            P("ctx", "ep"),
            P("ctx", "ep"),
            P("ctx", "ep"),
            P("ep", None, None),
            P("ctx", "ep"),
        ),
        check_vma=False,
    )
```

profile of v0, /device:TPU:2, one launch (start us, length us, event | category | flops | bytes accessed | tf_op | source)
XLA Modules:
  0.0 797.9 jit_solution(11163868636489932232)
XLA Ops:
  12.9 72.9 %all-gather.15.cloned.1.call-done = bf16[32,128,128]{2,1,0:T(8,128)(2,1)} async-done(((bf16[2,128,128]{2,1,0:T(8,128)(2,1)}), bf16[32,128,128]{2,1,0:T(8,128)(2,1)}) %all-gather.15.cloned.1.call-update) | async-done | bytes 1048592 | tf_op jit(solution)/shard_map/all_gather | solution.py:11
  88.5 14.3 %all_to_all.67 = bf16[32,20,96]{2,1,0:T(8,128)(2,1)S(1)} all-to-all(bf16[32,20,96]{2,1,0:T(8,128)(2,1)S(1)} %all_to_all.53), channel_id=1, replica_groups=mesh['ctx'=16,'ep'=32] {'ep'}, dimensions={0} | all-to-all | bytes 245760 | tf_op jit(solution)/shard_map/all_to_all | solution.py:128
  104.0 52.8 %all-gather.13.cloned.1.call-done = bf16[8192,96]{0,1:T(8,128)(2,1)} async-done(((bf16[512,96]{0,1:T(8,128)(2,1)}), bf16[8192,96]{0,1:T(8,128)(2,1)}) %all-gather.13.cloned.1.call-update) | async-done | bytes 1572880 | tf_op jit(solution)/shard_map/all_gather | solution.py:83
  156.8 59.4 %all-gather.11.cloned.1.call-done = bf16[128,8192]{0,1:T(8,128)(2,1)} async-done(((bf16[128,256]{0,1:T(8,128)(2,1)}), bf16[128,8192]{0,1:T(8,128)(2,1)}) %all-gather.11.cloned.1.call-update) | async-done | bytes 2097168 | tf_op jit(solution)/shard_map/all_gather | solution.py:85
  216.3 2.6 fusion.33
  219.5 23.3 %all_gather.34 = bf16[128,3072]{0,1:T(8,128)(2,1)S(1)} all-gather(bf16[128,96]{0,1:T(8,128)(2,1)S(1)} %fusion.33), channel_id=1, replica_groups=mesh['ctx'=16,'ep'=32] {'ep'}, dimensions={1}, use_global_device_ids=true | all-gather | bytes 811008 | tf_op jit(solution)/shard_map/all_gather | solution.py:100
  246.5 6.2 all-to-all-start.3
  252.7 38.8 %all-gather.21.cloned.1.call-done = bf16[16,20,3072]{2,1,0:T(8,128)(2,1)} async-done(((bf16[1,20,3072]{2,1,0:T(8,128)(2,1)}), bf16[16,20,3072]{2,1,0:T(8,128)(2,1)}) %all-gather.21.cloned.1.call-update) | async-done | bytes 1966096 | tf_op jit(solution)/shard_map/all_gather | solution.py:129
  295.7 67.7 %all-gather.19.cloned.1.call-done = bf16[16,20,3072]{2,1,0:T(8,128)(2,1)} async-done(((bf16[1,20,3072]{2,1,0:T(8,128)(2,1)}), bf16[16,20,3072]{2,1,0:T(8,128)(2,1)}) %all-gather.19.cloned.1.call-update) | async-done | bytes 1966096 | tf_op jit(solution)/shard_map/all_gather | solution.py:111
  373.4 52.9 %fusion.70 = (bf16[24,3072]{1,0:T(8,128)(2,1)}, bf16[24,3072]{1,0:T(8,128)(2,1)}) fusion(bf16[320,3072]{1,0:T(8,128)(2,1)S(1)} %convolution_convert_fusion, bf16[320,3072]{1,0:T(8,128)(2,1)} %fusion.2), kind=kCustom, calls=%all-reduce-scatter.2 | all-reduce-scatter fusion | flops 2359297 | bytes 4229120
  427.3 5.2 collective-permute-start
  432.5 6.7 collective-permute-start.1
  440.9 4.2 collective-permute-start.3
  445.1 5.4 collective-permute-start.4
  451.5 5.0 collective-permute-start.5
  463.6 7.5 all-to-all-start.2
  474.1 4.1 all-to-all-done.2
  480.7 60.3 %psum.14 = f32[128]{0:T(128)S(1)} all-reduce(f32[128]{0:T(128)} %get-tuple-element.145), channel_id=1, replica_groups=mesh['ctx'=16,'ep'=32] {'ep'}, use_global_device_ids=true, to_apply=%region_9.10 | all-reduce | flops 128 | bytes 1024 | tf_op jit(solution)/shard_map/psum | solution.py:146
  542.5 27.4 %all_gather.37 = bf16[128,3072]{0,1:T(8,128)(2,1)S(1)} all-gather(bf16[128,96]{0,1:T(8,128)(2,1)S(1)} %fusion.59), channel_id=1, replica_groups=mesh['ctx'=16,'ep'=32] {'ep'}, dimensions={1}, use_global_device_ids=true | all-gather | bytes 811008 | tf_op jit(solution)/shard_map/all_gather | solution.py:153
  575.5 5.6 all-to-all-start
  582.5 5.7 all-to-all-done
  589.1 117.0 %all-reduce.7.cloned.1.call-done = bf16[2,128,128]{1,2,0:T(8,128)(2,1)} async-done(((bf16[2,128,128]{1,2,0:T(8,128)(2,1)}), bf16[2,128,128]{1,2,0:T(8,128)(2,1)}) %all-reduce.7.cloned.1.call-update) | async-done | bytes 65552 | tf_op jit(solution)/shard_map/psum | solution.py:160
  707.7 67.6 %all-gather.17.cloned.1.call-done = bf16[32,128,128]{2,1,0:T(8,128)(2,1)} async-done(((bf16[2,128,128]{2,1,0:T(8,128)(2,1)}), bf16[32,128,128]{2,1,0:T(8,128)(2,1)}) %all-gather.17.cloned.1.call-update) | async-done | bytes 1048592 | tf_op jit(solution)/shard_map/all_gather | solution.py:11
  775.3 13.4 %while.23 = (s32[]{:T(128)}, f32[2,128,128]{2,1,0:T(8,128)S(1)}, s32[]{:T(128)}, bf16[16,2,128,128]{3,2,1,0:T(8,128)(2,1)}, s32[]{:T(128)}, /*index=5*/s32[]{:T(128)}, s32[]{:T(128)}, s32[]{:T(128)}) while((s32[]{:T(128)}, f32[2,128,128]{2,1,0:T(8,128)S(1)}, s32[]{:T(128)}, bf16[16,2,128,128]{3,2,1,0:T(8,128)(2,1)}, s32[]{:T(128)}, ...), condition=%wide.region_12.13_spmd, body=%wide.region_11.12_spmd.sunk | while | flops 65542 | bytes 327815 | solution.py:18
  (182 shorter events, 69.3 us)
Async XLA Ops:
  7.2 286.8 %copy-start = (bf16[1,192,3072]{2,1,0:T(8,128)(2,1)S(1)}, bf16[1,192,3072]{2,1,0:T(8,128)(2,1)}, u32[]{:S(2)}) copy-start(bf16[1,192,3072]{2,1,0:T(8,128)(2,1)} %param.32) | copy-start | bytes 3538948
  7.2 78.7 %copy-start.24 = (f32[2,128,128]{2,1,0:T(8,128)S(1)}, f32[2,128,128]{2,1,0:T(8,128)}, u32[]{:S(2)}) copy-start(f32[2,128,128]{2,1,0:T(8,128)} %param.22) | copy-start | bytes 393220
  7.2 78.6 %all-gather.15.cloned.1.call-start = ((), (), s32[]{:S(2)}) async-start(), calls=%async_computation.7 | async-start | bytes 1114112 | tf_op jit(solution)/shard_map/all_gather | solution.py:11
  8.3 77.5 %copy-start.16 = (bf16[128,256]{0,1:T(8,128)(2,1)}, bf16[128,256]{0,1:T(8,128)(2,1)S(1)}, u32[]{:S(2)}) copy-start(bf16[128,256]{0,1:T(8,128)(2,1)S(1)} %copy.182) | copy-start | bytes 196612
  10.0 76.3 %copy-start.18 = (bf16[128,256]{1,0:T(8,128)(2,1)S(1)}, bf16[128,256]{1,0:T(8,128)(2,1)}, u32[]{:S(2)}) copy-start(bf16[128,256]{1,0:T(8,128)(2,1)} %param.21) | copy-start | bytes 196612
  10.0 146.8 %all-gather.13.cloned.1.call-start = ((), (), s32[]{:S(2)}) async-start(), calls=%async_computation.5 | async-start | bytes 1671168 | tf_op jit(solution)/shard_map/all_gather | solution.py:83
  10.7 205.5 %all-gather.11.cloned.1.call-start = ((), (), s32[]{:S(2)}) async-start(), calls=%async_computation.4 | async-start | bytes 2162688 | tf_op jit(solution)/shard_map/all_gather | solution.py:85
  87.3 204.1 %all-gather.21.cloned.1.call-start = ((), (), s32[]{:S(2)}) async-start(), calls=%async_computation.10 | async-start | bytes 2506752 | tf_op jit(solution)/shard_map/all_gather | solution.py:129
  87.9 128.3 %copy-start.27 = (bf16[128,96]{0,1:T(8,128)(2,1)S(1)}, bf16[128,96]{0,1:T(8,128)(2,1)}, u32[]{:S(2)}) copy-start(bf16[128,96]{0,1:T(8,128)(2,1)} %param.25) | copy-start | bytes 73732
  103.7 259.7 %all-gather.19.cloned.1.call-start = ((), (), s32[]{:S(2)}) async-start(), calls=%async_computation.9 | async-start | bytes 2506752 | tf_op jit(solution)/shard_map/all_gather | solution.py:111
  246.5 217.2 %all-to-all-start.3 = ((bf16[32,256,96]{1,2,0:T(8,128)(2,1)}), bf16[32,256,96]{1,2,0:T(8,128)(2,1)}, u32[]{:S(2)}, u32[]{:S(2)}) async-start(bf16[32,256,96]{1,2,0:T(8,128)(2,1)} %bitcast.161), calls=%async_computation.3 | async-start | bytes 3145728 | tf_op jit(solution)/shard_map/all_to_all | solution.py:152
  427.3 31.1 %collective-permute-start = (bf16[24,3072]{1,0:T(8,128)(2,1)}, bf16[24,3072]{1,0:T(8,128)(2,1)S(1)}, u32[]{:S(2)}, u32[]{:S(2)}) collective-permute-start(bf16[24,3072]{1,0:T(8,128)(2,1)} %get-tuple-element.139), channel_id=1, source_target_pairs={{0,32},{32,64},{64,96},{96,128},{128,160},{160,192},{192,224},{224... | collective-permute-start | bytes 442376
  432.5 25.9 %collective-permute-start.1 = (bf16[24,3072]{1,0:T(8,128)(2,1)}, bf16[24,3072]{1,0:T(8,128)(2,1)S(1)}, u32[]{:S(2)}, u32[]{:S(2)}) collective-permute-start(bf16[24,3072]{1,0:T(8,128)(2,1)} %get-tuple-element.139), channel_id=1, source_target_pairs={{0,64},{32,96},{64,128},{96,160},{128,192},{160,224},{192,256},{22... | collective-permute-start | bytes 442376
  439.3 12.2 %collective-permute-start.2 = (bf16[12,3072]{1,0:T(8,128)(2,1)S(1)}, bf16[12,3072]{1,0:T(8,128)(2,1)S(1)}, u32[]{:S(2)}, u32[]{:S(2)}) collective-permute-start(bf16[12,3072]{1,0:T(8,128)(2,1)S(1)} %slice), channel_id=1, source_target_pairs={{0,96},{32,128},{64,160},{96,192},{128,224},{160,256},{192,288},{2... | collective-permute-start | bytes 221192
  440.9 20.0 %collective-permute-start.3 = (bf16[24,3072]{1,0:T(8,128)(2,1)}, bf16[24,3072]{1,0:T(8,128)(2,1)S(1)}, u32[]{:S(2)}, u32[]{:S(2)}) collective-permute-start(bf16[24,3072]{1,0:T(8,128)(2,1)} %get-tuple-element.140), channel_id=1, source_target_pairs={{0,32},{32,64},{64,96},{96,128},{128,160},{160,192},{192,224},{224... | collective-permute-start | bytes 442376
  445.1 15.8 %collective-permute-start.4 = (bf16[24,3072]{1,0:T(8,128)(2,1)}, bf16[24,3072]{1,0:T(8,128)(2,1)S(1)}, u32[]{:S(2)}, u32[]{:S(2)}) collective-permute-start(bf16[24,3072]{1,0:T(8,128)(2,1)} %get-tuple-element.140), channel_id=1, source_target_pairs={{0,64},{32,96},{64,128},{96,160},{128,192},{160,224},{192,256},{22... | collective-permute-start | bytes 442376
  451.5 9.4 %collective-permute-start.5 = (bf16[12,3072]{1,0:T(8,128)(2,1)S(1)}, bf16[12,3072]{1,0:T(8,128)(2,1)S(1)}, u32[]{:S(2)}, u32[]{:S(2)}) collective-permute-start(bf16[12,3072]{1,0:T(8,128)(2,1)S(1)} %slice.1), channel_id=1, source_target_pairs={{0,96},{32,128},{64,160},{96,192},{128,224},{160,256},{192,288},{2... | collective-permute-start | bytes 221192
  463.6 14.6 %all-to-all-start.2 = ((bf16[20,32,96]{2,0,1:T(8,128)(2,1)}), bf16[20,32,96]{2,0,1:T(8,128)(2,1)}, u32[]{:S(2)}, u32[]{:S(2)}) async-start(bf16[20,32,96]{2,0,1:T(8,128)(2,1)} %copy.119), calls=%async_computation.2 | async-start | bytes 393216 | tf_op jit(solution)/shard_map/all_to_all | solution.py:143
  471.7 98.2 %copy-start.8 = (f32[128,2,128]{0,2,1:T(8,128)S(1)}, f32[128,2,128]{0,2,1:T(8,128)}, u32[]{:S(2)}) copy-start(f32[128,2,128]{0,2,1:T(8,128)} %copy-done.7) | copy-start | bytes 393220
  572.4 133.8 %all-reduce.7.cloned.1.call-start = ((), (), s32[]{:S(2)}) async-start(), calls=%async_computation.6 | async-start | bytes 131072 | tf_op jit(solution)/shard_map/psum | solution.py:160
  572.9 202.4 %all-gather.17.cloned.1.call-start = ((), (), s32[]{:S(2)}) async-start(), calls=%async_computation.8 | async-start | bytes 1114112 | tf_op jit(solution)/shard_map/all_gather | solution.py:11
  575.5 12.6 %all-to-all-start = ((bf16[20,32,96]{2,0,1:T(8,128)(2,1)}), bf16[20,32,96]{2,0,1:T(8,128)(2,1)S(1)}, u32[]{:S(2)}, u32[]{:S(2)}) async-start(bf16[20,32,96]{2,0,1:T(8,128)(2,1)} %copy.114), calls=%async_computation | async-start | bytes 393216 | tf_op jit(solution)/shard_map/all_to_all | solution.py:123
  581.6 207.1 %copy-start.21 = (bf16[128,256]{1,0:T(8,128)(2,1)S(1)}, bf16[128,256]{1,0:T(8,128)(2,1)}, u32[]{:S(2)}) copy-start(bf16[128,256]{1,0:T(8,128)(2,1)} %param.20) | copy-start | bytes 196612
  588.2 201.1 %copy-start.23 = (bf16[2,128,128]{2,1,0:T(8,128)(2,1)S(1)}, bf16[2,128,128]{2,1,0:T(8,128)(2,1)}, u32[]{:S(2)}) copy-start(bf16[2,128,128]{2,1,0:T(8,128)(2,1)} %copy-done.22) | copy-start | bytes 196612
  (30 other events, 401.8 us)
Sparse Core Ops, SparseCore 0:
  10.7 75.1 all-gather.14
  87.9 68.8 all-gather.12
  160.5 55.6 all-gather.10
  218.2 73.1 all-gather.20
  293.4 69.9 all-gather.18
  575.2 130.9 all-reduce.6
  708.8 66.4 all-gather.16
where the time goes:
time: 800 us; the launch traced here: 798 us
  waiting for transfers between devices  488 us (61%)
  blocking collectives  178 us (22%)
  starting transfers between devices  47.7 us (6%)
  local copies, waits for them, and re-layouts  29.8 us (4%)
  matrix products  22.5 us (3%)
  other arithmetic  15.8 us (2%)
  between operations  15.6 us (2%)
    all_gather x2, waiting for transfers between devices, carried_in(): gathered = lax.all_gather(value.astype(jnp.bfloat16), axis)  141 us
    psum x1, waiting for transfers between devices, local(): lax.psum(state_part.astype(jnp.bfloat16), 'ctx').astype(jnp.float32)  117 us
    all_gather x1, waiting for transfers between devices, local(): portion = lax.all_gather(expert_in, 'ctx', axis=0, tiled=True)  67.7 us
    psum x1, blocking collectives, local(): inner_sum = lax.psum(jnp.sum(stream_f * scaled_grad, -1), 'ep')  60.3 us
    all_gather x1, waiting for transfers between devices, local(): lax.all_gather(normed_heads, 'ep', axis=1, tiled=True)  59.4 us
    unnamed x1, blocking collectives  52.9 us
    all_gather x1, waiting for transfers between devices, local(): w_cols = lax.all_gather(out_weight, 'ctx', axis=0, tiled=True)  52.8 us
    all_gather x1, waiting for transfers between devices, local(): lax.all_gather(grad_in, 'ctx', axis=0, tiled=True)  38.8 us
  transfers between devices with their start and end apart: 16, of which 9 were waited for; matrix products, arithmetic and copies ran while one was open for 12% of the time, Pallas kernels for 0%

commit v1 on v0

--- a/solution.py
+++ b/solution.py
@@ -143,7 +143,7 @@
     grad_back = lax.all_to_all(grad_half, "ep", split_axis=1, concat_axis=0, tiled=True)
     grad_model_in = jnp.dot(dest_picks, grad_back.astype(f32), precision=high)
     scaled_grad = grad_model_in * gain_cols
-    inner_sum = lax.psum(jnp.sum(stream_f * scaled_grad, -1), "ep")
+    inner_sum = jnp.sum(lax.all_gather(jnp.sum(stream_f * scaled_grad, -1), "ep"), axis=0)
     grad_stream = (
         grad_out
         + row_scale * scaled_grad

time: 800 us -> 756 us (0.945)
  blocking collectives: 178 us -> 134 us
    psum x1 -> x0, blocking collectives: 60.3 us -> none  [local(): inner_sum = lax.psum(jnp.sum(stream_f * scaled_grad, -1), 'ep')]
    all_gather x0 -> x1, blocking collectives: none -> 19.5 us  [local(): lax.all_gather(jnp.sum(stream_f * scaled_grad, -1), 'ep')]
where the time goes in v1:
time: 756 us; the launch traced here: 753 us
  waiting for transfers between devices  488 us (65%)
  blocking collectives  134 us (18%)
  starting transfers between devices  48.3 us (6%)
  local copies, waits for them, and re-layouts  29.8 us (4%)
  matrix products  21.9 us (3%)
  other arithmetic  15.8 us (2%)
  between operations  15.6 us (2%)
    all_gather x2, waiting for transfers between devices, carried_in(): gathered = lax.all_gather(value.astype(jnp.bfloat16), axis)  141 us
    psum x1, waiting for transfers between devices, local(): lax.psum(state_part.astype(jnp.bfloat16), 'ctx').astype(jnp.float32)  117 us
    all_gather x1, waiting for transfers between devices, local(): portion = lax.all_gather(expert_in, 'ctx', axis=0, tiled=True)  67.7 us
    all_gather x1, waiting for transfers between devices, local(): lax.all_gather(normed_heads, 'ep', axis=1, tiled=True)  59.4 us
    unnamed x1, blocking collectives  52.9 us
    all_gather x1, waiting for transfers between devices, local(): w_cols = lax.all_gather(out_weight, 'ctx', axis=0, tiled=True)  52.8 us
    all_gather x1, waiting for transfers between devices, local(): lax.all_gather(grad_in, 'ctx', axis=0, tiled=True)  38.8 us
    unnamed x6, starting transfers between devices  28.2 us
  transfers between devices with their start and end apart: 16, of which 9 were waited for; matrix products, arithmetic and copies ran while one was open for 12% of the time, Pallas kernels for 0%

profile of v1, /device:TPU:2, one launch (start us, length us, event | category | flops | bytes accessed | tf_op | source)
XLA Modules:
  0.0 753.4 jit_solution(8561460307433630551)
XLA Ops:
  12.9 72.9 %all-gather.17.cloned.1.call-done = bf16[32,128,128]{2,1,0:T(8,128)(2,1)} async-done(((bf16[2,128,128]{2,1,0:T(8,128)(2,1)}), bf16[32,128,128]{2,1,0:T(8,128)(2,1)}) %all-gather.17.cloned.1.call-update) | async-done | bytes 1048592 | tf_op jit(solution)/shard_map/all_gather | solution.py:11
  88.5 14.3 %all_to_all.67 = bf16[32,20,96]{2,1,0:T(8,128)(2,1)S(1)} all-to-all(bf16[32,20,96]{2,1,0:T(8,128)(2,1)S(1)} %all_to_all.53), channel_id=1, replica_groups=mesh['ctx'=16,'ep'=32] {'ep'}, dimensions={0} | all-to-all | bytes 245760 | tf_op jit(solution)/shard_map/all_to_all | solution.py:128
  104.0 52.8 %all-gather.15.cloned.1.call-done = bf16[8192,96]{0,1:T(8,128)(2,1)} async-done(((bf16[512,96]{0,1:T(8,128)(2,1)}), bf16[8192,96]{0,1:T(8,128)(2,1)}) %all-gather.15.cloned.1.call-update) | async-done | bytes 1572880 | tf_op jit(solution)/shard_map/all_gather | solution.py:83
  156.8 59.4 %all-gather.13.cloned.1.call-done = bf16[128,8192]{0,1:T(8,128)(2,1)} async-done(((bf16[128,256]{0,1:T(8,128)(2,1)}), bf16[128,8192]{0,1:T(8,128)(2,1)}) %all-gather.13.cloned.1.call-update) | async-done | bytes 2097168 | tf_op jit(solution)/shard_map/all_gather | solution.py:85
  216.3 2.6 fusion.33
  219.5 23.3 %all_gather.40 = bf16[128,3072]{0,1:T(8,128)(2,1)S(1)} all-gather(bf16[128,96]{0,1:T(8,128)(2,1)S(1)} %fusion.33), channel_id=1, replica_groups=mesh['ctx'=16,'ep'=32] {'ep'}, dimensions={1}, use_global_device_ids=true | all-gather | bytes 811008 | tf_op jit(solution)/shard_map/all_gather | solution.py:100
  246.5 6.2 all-to-all-start.3
  252.7 38.8 %all-gather.23.cloned.1.call-done = bf16[16,20,3072]{2,1,0:T(8,128)(2,1)} async-done(((bf16[1,20,3072]{2,1,0:T(8,128)(2,1)}), bf16[16,20,3072]{2,1,0:T(8,128)(2,1)}) %all-gather.23.cloned.1.call-update) | async-done | bytes 1966096 | tf_op jit(solution)/shard_map/all_gather | solution.py:129
  295.7 67.7 %all-gather.21.cloned.1.call-done = bf16[16,20,3072]{2,1,0:T(8,128)(2,1)} async-done(((bf16[1,20,3072]{2,1,0:T(8,128)(2,1)}), bf16[16,20,3072]{2,1,0:T(8,128)(2,1)}) %all-gather.21.cloned.1.call-update) | async-done | bytes 1966096 | tf_op jit(solution)/shard_map/all_gather | solution.py:111
  373.4 52.9 %fusion.70 = (bf16[24,3072]{1,0:T(8,128)(2,1)}, bf16[24,3072]{1,0:T(8,128)(2,1)}) fusion(bf16[320,3072]{1,0:T(8,128)(2,1)S(1)} %convolution_convert_fusion, bf16[320,3072]{1,0:T(8,128)(2,1)} %fusion.2), kind=kCustom, calls=%all-reduce-scatter.2 | all-reduce-scatter fusion | flops 2359297 | bytes 4229120
  427.3 5.2 collective-permute-start
  432.5 6.7 collective-permute-start.1
  440.9 4.2 collective-permute-start.3
  445.1 5.4 collective-permute-start.4
  451.5 5.0 collective-permute-start.5
  463.6 7.5 all-to-all-start.2
  474.1 4.1 all-to-all-done.2
  480.2 19.5 %all-gather.5 = f32[32,1,128]{2,1,0:T(1,128)S(1)} all-gather(f32[1,1,128]{2,1,0:T(1,128)S(1)} %bitcast.177), channel_id=3, replica_groups=mesh['ctx'=16,'ep'=32] {'ep'}, dimensions={0}, use_global_device_ids=true | all-gather | bytes 16896 | tf_op jit(solution)/shard_map/all_gather | solution.py:146
  501.1 23.6 %all_gather.45 = bf16[128,3072]{0,1:T(8,128)(2,1)S(1)} all-gather(bf16[128,96]{0,1:T(8,128)(2,1)S(1)} %fusion.59), channel_id=1, replica_groups=mesh['ctx'=16,'ep'=32] {'ep'}, dimensions={1}, use_global_device_ids=true | all-gather | bytes 811008 | tf_op jit(solution)/shard_map/all_gather | solution.py:153
  530.4 6.2 all-to-all-start
  538.0 5.7 all-to-all-done
  544.7 117.0 %all-reduce.7.cloned.1.call-done = bf16[2,128,128]{1,2,0:T(8,128)(2,1)} async-done(((bf16[2,128,128]{1,2,0:T(8,128)(2,1)}), bf16[2,128,128]{1,2,0:T(8,128)(2,1)}) %all-reduce.7.cloned.1.call-update) | async-done | bytes 65552 | tf_op jit(solution)/shard_map/psum | solution.py:160
  663.2 67.6 %all-gather.19.cloned.1.call-done = bf16[32,128,128]{2,1,0:T(8,128)(2,1)} async-done(((bf16[2,128,128]{2,1,0:T(8,128)(2,1)}), bf16[32,128,128]{2,1,0:T(8,128)(2,1)}) %all-gather.19.cloned.1.call-update) | async-done | bytes 1048592 | tf_op jit(solution)/shard_map/all_gather | solution.py:11
  730.8 13.4 %while.23 = (s32[]{:T(128)}, f32[2,128,128]{2,1,0:T(8,128)S(1)}, s32[]{:T(128)}, bf16[16,2,128,128]{3,2,1,0:T(8,128)(2,1)}, s32[]{:T(128)}, /*index=5*/s32[]{:T(128)}, s32[]{:T(128)}, s32[]{:T(128)}) while((s32[]{:T(128)}, f32[2,128,128]{2,1,0:T(8,128)S(1)}, s32[]{:T(128)}, bf16[16,2,128,128]{3,2,1,0:T(8,128)(2,1)}, s32[]{:T(128)}, ...), condition=%wide.region_12.13_spmd, body=%wide.region_11.12_spmd.sunk | while | flops 65542 | bytes 327815 | solution.py:18
  (183 shorter events, 68.8 us)
Async XLA Ops:
  7.2 286.8 %copy-start = (bf16[1,192,3072]{2,1,0:T(8,128)(2,1)S(1)}, bf16[1,192,3072]{2,1,0:T(8,128)(2,1)}, u32[]{:S(2)}) copy-start(bf16[1,192,3072]{2,1,0:T(8,128)(2,1)} %param.32) | copy-start | bytes 3538948
  7.2 78.7 %copy-start.24 = (f32[2,128,128]{2,1,0:T(8,128)S(1)}, f32[2,128,128]{2,1,0:T(8,128)}, u32[]{:S(2)}) copy-start(f32[2,128,128]{2,1,0:T(8,128)} %param.22) | copy-start | bytes 393220
  7.2 78.6 %all-gather.17.cloned.1.call-start = ((), (), s32[]{:S(2)}) async-start(), calls=%async_computation.7 | async-start | bytes 1114112 | tf_op jit(solution)/shard_map/all_gather | solution.py:11
  8.3 77.5 %copy-start.16 = (bf16[128,256]{0,1:T(8,128)(2,1)}, bf16[128,256]{0,1:T(8,128)(2,1)S(1)}, u32[]{:S(2)}) copy-start(bf16[128,256]{0,1:T(8,128)(2,1)S(1)} %copy.182) | copy-start | bytes 196612
  10.0 76.3 %copy-start.18 = (bf16[128,256]{1,0:T(8,128)(2,1)S(1)}, bf16[128,256]{1,0:T(8,128)(2,1)}, u32[]{:S(2)}) copy-start(bf16[128,256]{1,0:T(8,128)(2,1)} %param.21) | copy-start | bytes 196612
  10.0 146.8 %all-gather.15.cloned.1.call-start = ((), (), s32[]{:S(2)}) async-start(), calls=%async_computation.5 | async-start | bytes 1671168 | tf_op jit(solution)/shard_map/all_gather | solution.py:83
  10.7 205.5 %all-gather.13.cloned.1.call-start = ((), (), s32[]{:S(2)}) async-start(), calls=%async_computation.4 | async-start | bytes 2162688 | tf_op jit(solution)/shard_map/all_gather | solution.py:85
  11.7 74.7 %copy-start.12 = (bf16[128,256]{0,1:T(8,128)(2,1)}, bf16[128,256]{0,1:T(8,128)(2,1)S(1)}, u32[]{:S(2)}) copy-start(bf16[128,256]{0,1:T(8,128)(2,1)S(1)} %copy.145) | copy-start | bytes 196612
  87.3 204.1 %all-gather.23.cloned.1.call-start = ((), (), s32[]{:S(2)}) async-start(), calls=%async_computation.10 | async-start | bytes 2506752 | tf_op jit(solution)/shard_map/all_gather | solution.py:129
  87.9 128.3 %copy-start.27 = (bf16[128,96]{0,1:T(8,128)(2,1)S(1)}, bf16[128,96]{0,1:T(8,128)(2,1)}, u32[]{:S(2)}) copy-start(bf16[128,96]{0,1:T(8,128)(2,1)} %param.25) | copy-start | bytes 73732
  103.7 259.7 %all-gather.21.cloned.1.call-start = ((), (), s32[]{:S(2)}) async-start(), calls=%async_computation.9 | async-start | bytes 2506752 | tf_op jit(solution)/shard_map/all_gather | solution.py:111
  246.5 217.2 %all-to-all-start.3 = ((bf16[32,256,96]{1,2,0:T(8,128)(2,1)}), bf16[32,256,96]{1,2,0:T(8,128)(2,1)}, u32[]{:S(2)}, u32[]{:S(2)}) async-start(bf16[32,256,96]{1,2,0:T(8,128)(2,1)} %bitcast.162), calls=%async_computation.3 | async-start | bytes 3145728 | tf_op jit(solution)/shard_map/all_to_all | solution.py:152
  427.3 31.1 %collective-permute-start = (bf16[24,3072]{1,0:T(8,128)(2,1)}, bf16[24,3072]{1,0:T(8,128)(2,1)S(1)}, u32[]{:S(2)}, u32[]{:S(2)}) collective-permute-start(bf16[24,3072]{1,0:T(8,128)(2,1)} %get-tuple-element.139), channel_id=1, source_target_pairs={{0,32},{32,64},{64,96},{96,128},{128,160},{160,192},{192,224},{224... | collective-permute-start | bytes 442376
  432.5 25.9 %collective-permute-start.1 = (bf16[24,3072]{1,0:T(8,128)(2,1)}, bf16[24,3072]{1,0:T(8,128)(2,1)S(1)}, u32[]{:S(2)}, u32[]{:S(2)}) collective-permute-start(bf16[24,3072]{1,0:T(8,128)(2,1)} %get-tuple-element.139), channel_id=1, source_target_pairs={{0,64},{32,96},{64,128},{96,160},{128,192},{160,224},{192,256},{22... | collective-permute-start | bytes 442376
  439.3 12.2 %collective-permute-start.2 = (bf16[12,3072]{1,0:T(8,128)(2,1)S(1)}, bf16[12,3072]{1,0:T(8,128)(2,1)S(1)}, u32[]{:S(2)}, u32[]{:S(2)}) collective-permute-start(bf16[12,3072]{1,0:T(8,128)(2,1)S(1)} %slice), channel_id=1, source_target_pairs={{0,96},{32,128},{64,160},{96,192},{128,224},{160,256},{192,288},{2... | collective-permute-start | bytes 221192
  440.9 20.0 %collective-permute-start.3 = (bf16[24,3072]{1,0:T(8,128)(2,1)}, bf16[24,3072]{1,0:T(8,128)(2,1)S(1)}, u32[]{:S(2)}, u32[]{:S(2)}) collective-permute-start(bf16[24,3072]{1,0:T(8,128)(2,1)} %get-tuple-element.140), channel_id=1, source_target_pairs={{0,32},{32,64},{64,96},{96,128},{128,160},{160,192},{192,224},{224... | collective-permute-start | bytes 442376
  445.1 15.8 %collective-permute-start.4 = (bf16[24,3072]{1,0:T(8,128)(2,1)}, bf16[24,3072]{1,0:T(8,128)(2,1)S(1)}, u32[]{:S(2)}, u32[]{:S(2)}) collective-permute-start(bf16[24,3072]{1,0:T(8,128)(2,1)} %get-tuple-element.140), channel_id=1, source_target_pairs={{0,64},{32,96},{64,128},{96,160},{128,192},{160,224},{192,256},{22... | collective-permute-start | bytes 442376
  451.5 9.4 %collective-permute-start.5 = (bf16[12,3072]{1,0:T(8,128)(2,1)S(1)}, bf16[12,3072]{1,0:T(8,128)(2,1)S(1)}, u32[]{:S(2)}, u32[]{:S(2)}) collective-permute-start(bf16[12,3072]{1,0:T(8,128)(2,1)S(1)} %slice.1), channel_id=1, source_target_pairs={{0,96},{32,128},{64,160},{96,192},{128,224},{160,256},{192,288},{2... | collective-permute-start | bytes 221192
  463.6 14.6 %all-to-all-start.2 = ((bf16[20,32,96]{2,0,1:T(8,128)(2,1)}), bf16[20,32,96]{2,0,1:T(8,128)(2,1)}, u32[]{:S(2)}, u32[]{:S(2)}) async-start(bf16[20,32,96]{2,0,1:T(8,128)(2,1)} %copy.119), calls=%async_computation.2 | async-start | bytes 393216 | tf_op jit(solution)/shard_map/all_to_all | solution.py:143
  527.3 134.4 %all-reduce.7.cloned.1.call-start = ((), (), s32[]{:S(2)}) async-start(), calls=%async_computation.6 | async-start | bytes 131072 | tf_op jit(solution)/shard_map/psum | solution.py:160
  527.8 203.0 %all-gather.19.cloned.1.call-start = ((), (), s32[]{:S(2)}) async-start(), calls=%async_computation.8 | async-start | bytes 1114112 | tf_op jit(solution)/shard_map/all_gather | solution.py:11
  530.4 13.3 %all-to-all-start = ((bf16[20,32,96]{2,0,1:T(8,128)(2,1)}), bf16[20,32,96]{2,0,1:T(8,128)(2,1)S(1)}, u32[]{:S(2)}, u32[]{:S(2)}) async-start(bf16[20,32,96]{2,0,1:T(8,128)(2,1)} %copy.114), calls=%async_computation | async-start | bytes 393216 | tf_op jit(solution)/shard_map/all_to_all | solution.py:123
  537.1 207.1 %copy-start.21 = (bf16[128,256]{1,0:T(8,128)(2,1)S(1)}, bf16[128,256]{1,0:T(8,128)(2,1)}, u32[]{:S(2)}) copy-start(bf16[128,256]{1,0:T(8,128)(2,1)} %param.20) | copy-start | bytes 196612
  543.7 201.1 %copy-start.23 = (bf16[2,128,128]{2,1,0:T(8,128)(2,1)S(1)}, bf16[2,128,128]{2,1,0:T(8,128)(2,1)}, u32[]{:S(2)}) copy-start(bf16[2,128,128]{2,1,0:T(8,128)(2,1)} %copy-done.22) | copy-start | bytes 196612
  (30 other events, 382.6 us)
Sparse Core Ops, SparseCore 0:
  10.7 75.1 all-gather.16
  87.9 68.8 all-gather.14
  160.5 55.6 all-gather.12
  218.2 73.1 all-gather.22
  293.4 69.9 all-gather.20
  530.1 131.5 all-reduce.6
  664.3 66.4 all-gather.18
